TPU v7x, 256 devices: a whole 4x4x8 slice. The times are simulated.
256 devices in a mesh: tiles: 64 (over y, z, core), cols: 4 (over x).
Axes of the slice: x: 4, y: 4, z: 8, core: 2. Of those that a mesh axis runs over, the one named last changes fastest.
Arguments:
- cov_blocks: bfloat16 [1024, 8, 256, 256], P('tiles', None, 'cols'), may hold values from -1 to 5, as said below
- neighbours: int32 [1024, 8], P('tiles'), may hold values from 0 to 1023, as said below
- voxel_mask: int32 [1024, 256], P('tiles', 'cols'), may hold values 0 or 1
- start_block: bfloat16 [128, 1024, 256], P('cols', 'tiles'), may hold values from -6 to 6
- overdensity: float32 [1024, 256], P('tiles', 'cols'), may hold values from -12 to 12
Outputs:
- basis_next: bfloat16 [128, 1024, 256], P('cols', 'tiles')
- coeffs: float32 [3, 128], replicated
Inputs may be any that keep to these rules, and one draw needn't show every extreme that they name: Slot 0 names the tile itself. Every other entry names another tile at most 3 away, counting cyclically (tile 1024 - 1 is next to tile 0), and some entry is exactly 3 away. If neighbours[i, k] = j then neighbours[j, k] = i. cov_blocks[j, k] is the transpose of cov_blocks[i, k] where neighbours[i, k] = j; the blocks of slot 0 are symmetric.
All inputs are finite; a program needn't handle non-finite values. No bound on the sum of `voxel_mask` on one device may be relied on, other than what follows from the above.
Results may differ from a plain program's by a relative error of at most 0.01.
The roundings to bfloat16 on the way count: a program that leaves them out, or rounds other values in their place, can miss the bound.
Values may be sent and summed in bfloat16 or wider, within the bound.
No kernel may reach another device: no remote copies, remote signals or barrier semaphores. Data moves between devices by JAX's collectives and lax.ppermute only.
A program may use at most 64 MiB of HBM per device.

v0:
```python
import math

import jax
import jax.numpy as jnp
from jax import lax
from jax.sharding import PartitionSpec as P

REACH = 3


def with_halo(cells, sides, width):
    for axis, dim in sides:
        count = lax.axis_size(axis)
        head = lax.slice_in_dim(cells, 0, width, axis=dim)
        tail = lax.slice_in_dim(cells, cells.shape[dim] - width, cells.shape[dim], axis=dim)
        cells = jnp.concatenate(
            [
                lax.ppermute(tail, axis, [(i, (i + 1) % count) for i in range(count)]),
                cells,
                lax.ppermute(head, axis, [((i + 1) % count, i) for i in range(count)]),
            ],
            axis=dim,
        )
    return cells


def orthonormal(work):
    gram = lax.psum(jnp.dot(work, work.T, preferred_element_type=jnp.float32), ("tiles", "cols"))
    lower = jnp.linalg.cholesky(gram)
    identity = jnp.eye(work.shape[0], dtype=jnp.float32)
    inverse = jax.scipy.linalg.solve_triangular(lower, identity, lower=True).astype(jnp.bfloat16)
    return jnp.dot(inverse, work, preferred_element_type=jnp.float32)


def projection(basis_flat, density):
    return jnp.sum(basis_flat.astype(jnp.float32) * density[None, :], axis=1)


def settle(terms):
    return lax.psum(terms, ("tiles", "cols"))


def fold_slots(total, piece, cov_blocks, local_index):
    for slot in range(cov_blocks.shape[1]):
        picked = jnp.take(piece, local_index[:, slot], axis=1)
        blocks = cov_blocks[:, slot]
        total = total + jnp.einsum(
            "iuv,biv->biu", blocks, picked, preferred_element_type=jnp.float32
        )
    return total


def local(cov_blocks, neighbours, voxel_mask, start_block, overdensity):
    tiles_here = neighbours.shape[0]
    voxels_here = voxel_mask.shape[1]
    voxels_all = cov_blocks.shape[3]
    cycle_size = tiles_here * lax.axis_size("tiles")
    first_tile = lax.axis_index("tiles") * tiles_here
    local_index = jnp.mod(neighbours - first_tile + REACH, cycle_size)
    mask_values = voxel_mask.astype(jnp.float32)
    density = overdensity.reshape(-1)
    start_cube = lax.all_to_all(start_block, "cols", split_axis=2, concat_axis=0, tiled=True)
    count = start_cube.shape[0]
    start_flat = (
        (start_cube.astype(jnp.float32) * mask_values[None]).astype(jnp.bfloat16).reshape(count, -1)
    )
    basis_now = orthonormal(start_flat).astype(jnp.bfloat16)
    basis_old = None
    found = []
    pending = projection(basis_now, density)
    found.append(settle(pending))
    rotated = None
    for lanczos_round in range(2):
        image_count = basis_now.shape[0]
        basis_cube = basis_now.reshape(image_count, tiles_here, voxels_here)
        empty = jnp.zeros((image_count, tiles_here, voxels_here), jnp.float32)
        gathered = lax.all_gather(basis_cube, "cols", axis=2, tiled=True)
        padded = with_halo(gathered, (("tiles", 1),), REACH)
        total = fold_slots(empty, padded, cov_blocks, local_index)
        image = (total * mask_values[None]).astype(jnp.bfloat16).reshape(image_count, -1)
        if basis_old is None:
            stacked = basis_now
        else:
            stacked = jnp.concatenate([basis_now, basis_old], axis=0)
        local_sums = jnp.dot(stacked, image.T, preferred_element_type=jnp.float32)
        sums = lax.psum(local_sums, ("tiles", "cols"))
        along = sums[:count].astype(jnp.bfloat16)
        resid = image.astype(jnp.float32) - jnp.dot(
            along.T, basis_now, preferred_element_type=jnp.float32
        )
        if basis_old is not None:
            back = sums[count:].astype(jnp.bfloat16)
            resid = resid - jnp.dot(back.T, basis_old, preferred_element_type=jnp.float32)
        rotated = orthonormal(resid.astype(jnp.bfloat16))
        basis_old, basis_now = (basis_now, rotated.astype(jnp.bfloat16))
        pending = projection(basis_now, density)
        found.append(settle(pending))
    coeffs = jnp.stack(found)
    scaled = (rotated * math.sqrt(cycle_size * voxels_all)).astype(jnp.bfloat16)
    scaled = scaled.reshape(count, tiles_here, voxels_here)
    basis_next = lax.all_to_all(scaled, "cols", split_axis=0, concat_axis=2, tiled=True)
    return (basis_next, coeffs)


def solution(mesh):
    return jax.shard_map(
        local,
        mesh=mesh,
        in_specs=(
            P("tiles", None, "cols", None),
            P("tiles", None),
            P("tiles", "cols"),
            P("cols", "tiles", None),
            P("tiles", "cols"),
        ),
        out_specs=(P("cols", "tiles", None), P()),
        check_vma=False,
    )
```

profile of v0, /device:TPU:8, one launch (start us, length us, event | category | flops | bytes accessed | tf_op | source)
XLA Modules:
  0.0 1188.2 jit_solution(6091634544763093636)
XLA Ops:
  7.2 2.4 copy.138
  9.5 1.7 reshape.230
  11.2 4.3 all-to-all-start
  16.2 6.0 all-to-all-done
  25.3 241.3 %all-reduce.6.cloned.1.call-done = f32[128,128]{0,1:T(8,128)} async-done(((f32[128,128]{0,1:T(8,128)}), f32[128,128]{0,1:T(8,128)}) %all-reduce.6.cloned.1.call-update) | async-done | bytes 65552 | tf_op jit(solution)/shard_map/psum | solution.py:28
  268.4 11.7 cholesky.59
  281.5 9.8 custom-call.7
  293.0 24.0 %all-gather.3.cloned.1.call-done = bf16[128,16,256]{0,1,2:T(8,128)(2,1)} async-done(((bf16[128,16,64]{0,1,2:T(8,128)(2,1)}), bf16[128,16,256]{0,1,2:T(8,128)(2,1)}) %all-gather.3.cloned.1.call-update) | async-done | bytes 1048592 | tf_op jit(solution)/shard_map/all_gather | solution.py:77
  318.7 13.1 %collective-permute-start = (bf16[128,3,256]{2,0,1:T(8,128)(2,1)S(1)}, bf16[128,3,256]{2,0,1:T(8,128)(2,1)S(1)}, u32[]{:S(2)}, u32[]{:S(2)}) collective-permute-start(bf16[128,3,256]{2,0,1:T(8,128)(2,1)S(1)} %get-tuple-element.29), channel_id=1, source_target_pairs={{0,4},{4,8},{8,12},{12,16},{16,20},{20,24},{24,28},{28,32},{32,36}... | collective-permute-start | bytes 589832 | tf_op jit(solution)/shard_map/ppermute | solution.py:18
  331.7 3.8 collective-permute-start.1
  335.6 3.3 collective-permute-done
  340.7 1.6 gather_fusion
  351.0 2.1 fusion.21
  353.1 2.1 convolution_add_fusion.13
  355.2 1.7 convolution_add_fusion.12
  360.2 77.2 %psum.57 = bf16[128,128]{1,0:T(8,128)(2,1)S(1)} all-reduce(f32[128,128]{1,0:T(8,128)S(1)} %fusion.149), channel_id=1, replica_groups=mesh['tiles'=64,'cols'=4] {'tiles','cols'}, use_global_device_ids=true, to_apply=%region_3.7 | all-reduce | flops 16384 | bytes 98304 | tf_op jit(solution)/shard_map/psum | solution.py:86
  438.6 237.4 %all-reduce.8.cloned.1.call-done = f32[128,128]{0,1:T(8,128)} async-done(((f32[128,128]{0,1:T(8,128)}), f32[128,128]{0,1:T(8,128)}) %all-reduce.8.cloned.1.call-update) | async-done | bytes 65552 | tf_op jit(solution)/shard_map/psum | solution.py:28
  677.7 11.7 cholesky.70
  690.8 9.8 custom-call.8
  702.3 24.0 %all-gather.5.cloned.1.call-done = bf16[128,16,256]{0,1,2:T(8,128)(2,1)} async-done(((bf16[128,16,64]{0,1,2:T(8,128)(2,1)}), bf16[128,16,256]{0,1,2:T(8,128)(2,1)}) %all-gather.5.cloned.1.call-update) | async-done | bytes 1048592 | tf_op jit(solution)/shard_map/all_gather | solution.py:77
  728.1 3.8 collective-permute-start.3
  731.9 3.3 collective-permute-done.2
  737.0 1.6 gather_fusion.8
  747.3 2.1 fusion.12
  749.4 2.1 convolution_add_fusion.6
  751.6 1.7 convolution_add_fusion.5
  756.6 77.4 %all-reduce.11 = bf16[256,128]{1,0:T(8,128)(2,1)S(1)} all-reduce(f32[256,128]{1,0:T(8,128)S(1)} %fusion.56), channel_id=1, replica_groups=mesh['tiles'=64,'cols'=4] {'tiles','cols'}, use_global_device_ids=true, to_apply=%region_5.9 | all-reduce | flops 32768 | bytes 196608 | tf_op jit(solution)/shard_map/psum | solution.py:86
  835.5 237.5 %all-reduce.10.cloned.1.call-done = f32[128,128]{0,1:T(8,128)} async-done(((f32[128,128]{0,1:T(8,128)}), f32[128,128]{0,1:T(8,128)}) %all-reduce.10.cloned.1.call-update) | async-done | bytes 65552 | tf_op jit(solution)/shard_map/psum | solution.py:28
  1074.8 11.7 cholesky.81
  1087.9 9.8 custom-call.9
  1100.0 3.8 all-to-all-start.1
  1103.8 75.0 %all-reduce = (f32[1,128]{1,0:T(1,128)S(1)}, f32[1,128]{1,0:T(1,128)S(1)}, f32[1,128]{1,0:T(1,128)S(1)}) all-reduce(f32[1,128]{1,0:T(1,128)S(1)} %bitcast.212, f32[1,128]{1,0:T(1,128)S(1)} %bitcast.211, f32[1,128]{1,0:T(1,128)S(1)} %bitcast.210), channel_id=1, replica_groups=mesh['tiles'=64,'cols'=4] {'tiles','cols'}, use_global_device_ids=true, to_apply=%region_12.16 | all-reduce | flops 384 | bytes 3072 | tf_op jit(solution)/shard_map/psum | solution.py:40
  (127 shorter events, 54.3 us)
Async XLA Ops:
  11.2 11.0 all-to-all-start
  15.5 251.1 %all-reduce.6.cloned.1.call-start = ((), (), s32[]{:S(2)}) async-start(), calls=%async_computation.2 | async-start | bytes 131072 | tf_op jit(solution)/shard_map/psum | solution.py:28
  22.7 270.3 %copy-start.11 = (s32[16,8]{0,1:T(8,128)S(1)}, s32[16,8]{0,1:T(8,128)}, u32[]{:S(2)}) copy-start(s32[16,8]{0,1:T(8,128)} %param.11) | copy-start | bytes 1540
  24.9 292.1 %all-gather.3.cloned.1.call-start = ((), (), s32[]{:S(2)}) async-start(), calls=%async_computation.3 | async-start | bytes 1310720 | tf_op jit(solution)/shard_map/all_gather | solution.py:77
  292.9 383.1 %all-reduce.8.cloned.1.call-start = ((), (), s32[]{:S(2)}) async-start(), calls=%async_computation.4 | async-start | bytes 131072 | tf_op jit(solution)/shard_map/psum | solution.py:28
  318.7 20.3 %collective-permute-start = (bf16[128,3,256]{2,0,1:T(8,128)(2,1)S(1)}, bf16[128,3,256]{2,0,1:T(8,128)(2,1)S(1)}, u32[]{:S(2)}, u32[]{:S(2)}) collective-permute-start(bf16[128,3,256]{2,0,1:T(8,128)(2,1)S(1)} %get-tuple-element.29), channel_id=1, source_target_pairs={{0,4},{4,8},{8,12},{12,16},{16,20},{20,24},{24,28},{28,32},{32,36}... | collective-permute-start | bytes 589832 | tf_op jit(solution)/shard_map/ppermute | solution.py:18
  331.7 7.2 collective-permute-start.1
  350.9 4.3 copy-start.9
  351.0 6.0 copy-start.8
  351.0 6.0 copy-start.12
  353.0 4.5 copy-start.7
  355.2 2.9 copy-start.6
  356.9 1.7 copy-start.4
  438.5 287.8 %all-gather.5.cloned.1.call-start = ((), (), s32[]{:S(2)}) async-start(), calls=%async_computation.5 | async-start | bytes 1310720 | tf_op jit(solution)/shard_map/all_gather | solution.py:77
  702.2 370.8 %all-reduce.10.cloned.1.call-start = ((), (), s32[]{:S(2)}) async-start(), calls=%async_computation.6 | async-start | bytes 131072 | tf_op jit(solution)/shard_map/psum | solution.py:28
  728.0 7.3 collective-permute-start.2
  728.1 7.2 collective-permute-start.3
  747.3 4.3 copy-start.5
  747.3 6.0 copy-start.3
  747.3 6.0 copy-start.13
  749.4 4.5 copy-start.2
  751.5 2.9 copy-start.1
  753.3 1.7 copy-start
  755.6 79.9 %copy-start.10 = (f32[16,64]{1,0:T(8,128)S(1)}, f32[16,64]{1,0:T(8,128)}, u32[]{:S(2)}) copy-start(f32[16,64]{1,0:T(8,128)} %param.14) | copy-start | bytes 12292
  1100.0 79.4 %all-to-all-start.1 = ((bf16[4,2,16384]{2,1,0:T(2,128)(2,1)}), bf16[4,2,16384]{2,1,0:T(2,128)(2,1)S(1)}, u32[]{:S(2)}, u32[]{:S(2)}) async-start(bf16[4,2,16384]{2,1,0:T(2,128)(2,1)} %reshape.232), calls=%async_computation.1 | async-start | bytes 524288 | tf_op jit(solution)/shard_map/all_to_all | solution.py:101
Sparse Core Ops, SparseCore 0:
  25.0 241.6 all-reduce.5
  293.0 23.9 all-gather.2
  438.7 237.2 all-reduce.7
  702.3 23.9 all-gather.4
  835.5 237.4 all-reduce.9
where the time goes:
time: 1200 us; the launch traced here: 1190 us
  waiting for transfers between devices  777 us (65%)
  blocking collectives  230 us (19%)
  other arithmetic  72.9 us (6%)
  local copies, waits for them, and re-layouts  41.8 us (3%)
  starting transfers between devices  29.1 us (2%)
  matrix products  23 us (2%)
  between operations  14.8 us (1%)
    psum x3, waiting for transfers between devices, orthonormal(): lax.psum(jnp.dot(work, work.T, preferred_element_type=jnp.float32), ('til...  716 us
    psum x2, blocking collectives, local(): sums = lax.psum(local_sums, ('tiles', 'cols'))  155 us
    psum x1, blocking collectives, settle(): return lax.psum(terms, ('tiles', 'cols'))  75 us
    all_gather x2, waiting for transfers between devices, local(): gathered = lax.all_gather(basis_cube, 'cols', axis=2, tiled=True)  48 us
    another operation x9, other arithmetic, orthonormal(): lower = jnp.linalg.cholesky(gram)  37.2 us
    another operation x6, other arithmetic, orthonormal(): jax.scipy.linalg.solve_triangular(lower, identity, lower=True)  31.4 us
  transfers between devices with their start and end apart: 11, of which 8 were waited for; matrix products, arithmetic and copies ran while one was open for 0% of the time, Pallas kernels for 0%

commit v1 on v0

--- a/solution.py
+++ b/solution.py
@@ -24,8 +24,55 @@
     return cells
 
 
+def pair_step(x, axis, count, stride):
+    perm = [(i, i ^ stride) for i in range(count)]
+    return x + lax.ppermute(x, axis, perm)
+
+
+def group_step(x, axis, count, stride, size):
+    me = (lax.axis_index(axis) // stride) % size
+    vals = [x]
+    for shift in range(1, size):
+        perm = []
+        for i in range(count):
+            digit = (i // stride) % size
+            perm.append((i, i + (((digit + shift) % size) - digit) * stride))
+        vals.append(lax.ppermute(x, axis, perm))
+    ordered = jnp.take(jnp.stack(vals), (me - jnp.arange(size)) % size, axis=0)
+    return jnp.sum(ordered, axis=0)
+
+
+def plan_of(count):
+    stages = []
+    stride = 1
+    pair_next = count > 4
+    while stride < count:
+        if not pair_next and count // stride >= 4:
+            stages.append(("group", stride, 4))
+            stride *= 4
+        else:
+            stages.append(("pair", stride, 2))
+            stride *= 2
+        pair_next = not pair_next
+    return stages
+
+
+def all_sum(x, axes=("cols", "tiles")):
+    for axis in axes:
+        count = lax.axis_size(axis)
+        if count & (count - 1):
+            x = lax.psum(x, axis)
+            continue
+        for kind, stride, size in plan_of(count):
+            if kind == "pair":
+                x = pair_step(x, axis, count, stride)
+            else:
+                x = group_step(x, axis, count, stride, size)
+    return x
+
+
 def orthonormal(work):
-    gram = lax.psum(jnp.dot(work, work.T, preferred_element_type=jnp.float32), ("tiles", "cols"))
+    gram = all_sum(jnp.dot(work, work.T, preferred_element_type=jnp.float32))
     lower = jnp.linalg.cholesky(gram)
     identity = jnp.eye(work.shape[0], dtype=jnp.float32)
     inverse = jax.scipy.linalg.solve_triangular(lower, identity, lower=True).astype(jnp.bfloat16)
@@ -34,10 +81,6 @@
 
 def projection(basis_flat, density):
     return jnp.sum(basis_flat.astype(jnp.float32) * density[None, :], axis=1)
-
-
-def settle(terms):
-    return lax.psum(terms, ("tiles", "cols"))
 
 
 def fold_slots(total, piece, cov_blocks, local_index):
@@ -68,7 +111,6 @@
     basis_old = None
     found = []
     pending = projection(basis_now, density)
-    found.append(settle(pending))
     rotated = None
     for lanczos_round in range(2):
         image_count = basis_now.shape[0]
@@ -83,18 +125,19 @@
         else:
             stacked = jnp.concatenate([basis_now, basis_old], axis=0)
         local_sums = jnp.dot(stacked, image.T, preferred_element_type=jnp.float32)
-        sums = lax.psum(local_sums, ("tiles", "cols"))
+        sums = all_sum(jnp.concatenate([local_sums, pending[None]], axis=0))
+        found.append(sums[-1])
         along = sums[:count].astype(jnp.bfloat16)
         resid = image.astype(jnp.float32) - jnp.dot(
             along.T, basis_now, preferred_element_type=jnp.float32
         )
         if basis_old is not None:
-            back = sums[count:].astype(jnp.bfloat16)
+            back = sums[count : 2 * count].astype(jnp.bfloat16)
             resid = resid - jnp.dot(back.T, basis_old, preferred_element_type=jnp.float32)
         rotated = orthonormal(resid.astype(jnp.bfloat16))
         basis_old, basis_now = (basis_now, rotated.astype(jnp.bfloat16))
         pending = projection(basis_now, density)
-        found.append(settle(pending))
+    found.append(all_sum(pending))
     coeffs = jnp.stack(found)
     scaled = (rotated * math.sqrt(cycle_size * voxels_all)).astype(jnp.bfloat16)
     scaled = scaled.reshape(count, tiles_here, voxels_here)

time: 1200 us -> 471 us (0.39)
  waiting for transfers between devices: 777 us -> 166 us
  blocking collectives: 230 us -> 0 us
  starting transfers between devices: 29.1 us -> 137 us
    psum x3 -> x0, waiting for transfers between devices: 716 us -> none  [orthonormal(): lax.psum(jnp.dot(work, work.T, preferred_element_type=jnp.float32), ('til...]
    psum x3 -> x0, blocking collectives: 230 us -> none  [the longest x2 155 us: local(): sums = lax.psum(local_sums, ('tiles', 'cols'))]
    ppermute x0 -> x66, starting transfers between devices: none -> 120 us  [the longest x54 92.1 us: group_step(): vals.append(lax.ppermute(x, axis, perm))]
    ppermute x0 -> x66, waiting for transfers between devices: none -> 95.8 us  [the longest x54 65.2 us: group_step(): vals.append(lax.ppermute(x, axis, perm))]
    ppermute x2, starting transfers between devices: 13.1 us -> 0.17 us  [with_halo(): lax.ppermute(tail, axis, [(i, (i + 1) % count) for i in range(count)])]
  transfers between devices with their start and end apart: 11 -> 74, of which waited for: 8 -> 57; matrix products, arithmetic and copies ran while one was open for 0% -> 1% of each run, Pallas kernels for 0% -> 0%
where the time goes in v1:
time: 471 us; the launch traced here: 462 us
  waiting for transfers between devices  166 us (35%)
  starting transfers between devices  137 us (29%)
  other arithmetic  72.8 us (15%)
  local copies, waits for them, and re-layouts  50.1 us (11%)
  matrix products  21.2 us (5%)
  between operations  15.3 us (3%)
    ppermute x54, starting transfers between devices, group_step(): vals.append(lax.ppermute(x, axis, perm))  92.1 us
    ppermute x54, waiting for transfers between devices, group_step(): vals.append(lax.ppermute(x, axis, perm))  65.2 us
    all_gather x2, waiting for transfers between devices, local(): gathered = lax.all_gather(basis_cube, 'cols', axis=2, tiled=True)  53.5 us
    another operation x9, other arithmetic, orthonormal(): lower = jnp.linalg.cholesky(gram)  37.2 us
    another operation x6, other arithmetic, orthonormal(): jax.scipy.linalg.solve_triangular(lower, identity, lower=True)  31.4 us
    ppermute x12, waiting for transfers between devices, pair_step(): return x + lax.ppermute(x, axis, perm)  30.6 us
    ppermute x12, starting transfers between devices, pair_step(): return x + lax.ppermute(x, axis, perm)  28.4 us
    gather x16, local copies, waits for them, and re-layouts, fold_slots(): picked = jnp.take(piece, local_index[:, slot], axis=1)  23.6 us
  transfers between devices with their start and end apart: 74, of which 57 were waited for; matrix products, arithmetic and copies ran while one was open for 1% of the time, Pallas kernels for 0%

profile of v1, /device:TPU:8, one launch (start us, length us, event | category | flops | bytes accessed | tf_op | source)
XLA Modules:
  0.0 462.4 jit_solution(13479169176730320562)
XLA Ops:
  11.2 4.3 all-to-all-start
  17.1 5.1 %all-to-all-done = bf16[4,2,16384]{2,1,0:T(2,128)(2,1)S(1)} async-done(((bf16[4,2,16384]{2,1,0:T(2,128)(2,1)}), bf16[4,2,16384]{2,1,0:T(2,128)(2,1)S(1)}, u32[]{:S(2)}, u32[]{:S(2)}) %all-to-all-start) | async-done | bytes 262176 | tf_op jit(solution)/shard_map/all_to_all | solution.py:105
  35.3 3.3 collective-permute-start.5
  44.5 5.8 %collective-permute-start.7 = (f32[128,128]{1,0:T(8,128)S(1)}, f32[128,128]{1,0:T(8,128)S(1)}, u32[]{:S(2)}, u32[]{:S(2)}) collective-permute-start(f32[128,128]{1,0:T(8,128)S(1)} %select_reduce_fusion.13), channel_id=1, source_target_pairs={{0,32},{4,36},{8,40},{12,44},{16,48},{20,52},{24,56},{28,60},{32,0... | collective-permute-start | bytes 196616 | tf_op jit(solution)/shard_map/ppermute | solution.py:29
  61.3 11.7 %cholesky.59 = f32[128,128]{1,0:T(8,128)S(1)} custom-call(f32[128,128]{1,0:T(8,128)S(1)} %fusion.122), custom_call_target="Cholesky" | custom-call | tf_op jit(solution)/shard_map/jit(cholesky)/cholesky | solution.py:76
  74.3 9.8 %custom-call.7 = f32[1,128,128]{1,2,0:T(8,128)S(1)} custom-call(f32[1,128,128]{2,1,0:T(8,128)S(1)} %fusion.114), custom_call_target="InvertDiagBlocksLowerTriangular" | custom-call | tf_op jit(solution)/shard_map/jit(_solve_triangular)/triangular_solve | solution.py:78
  85.9 29.2 %all-gather.3.cloned.1.call-done = bf16[128,16,256]{0,1,2:T(8,128)(2,1)} async-done(((bf16[128,16,64]{0,1,2:T(8,128)(2,1)}), bf16[128,16,256]{0,1,2:T(8,128)(2,1)}) %all-gather.3.cloned.1.call-update) | async-done | bytes 1048592 | tf_op jit(solution)/shard_map/all_gather | solution.py:119
  116.9 4.0 collective-permute-start.12
  154.9 4.1 collective-permute-start.18
  165.2 4.1 collective-permute-start.20
  169.3 4.9 %collective-permute-done.20 = f32[129,128]{1,0:T(8,128)S(1)} collective-permute-done((f32[129,128]{1,0:T(8,128)S(1)}, f32[129,128]{1,0:T(8,128)S(1)}, u32[]{:S(2)}, u32[]{:S(2)}) %collective-permute-start.20) | collective-permute-done | bytes 66080 | tf_op jit(solution)/shard_map/ppermute | solution.py:29
  203.9 3.9 collective-permute-start.31
  207.8 5.1 %collective-permute-done.31 = f32[128,128]{1,0:T(8,128)S(1)} collective-permute-done((f32[128,128]{1,0:T(8,128)S(1)}, f32[128,128]{1,0:T(8,128)S(1)}, u32[]{:S(2)}, u32[]{:S(2)}) %collective-permute-start.31) | collective-permute-done | bytes 65568 | tf_op jit(solution)/shard_map/ppermute | solution.py:29
  222.2 11.7 %cholesky.70 = f32[128,128]{1,0:T(8,128)S(1)} custom-call(f32[128,128]{1,0:T(8,128)S(1)} %fusion.120), custom_call_target="Cholesky" | custom-call | tf_op jit(solution)/shard_map/jit(cholesky)/cholesky | solution.py:76
  235.3 9.8 %custom-call.8 = f32[1,128,128]{1,2,0:T(8,128)S(1)} custom-call(f32[1,128,128]{2,1,0:T(8,128)S(1)} %fusion.115), custom_call_target="InvertDiagBlocksLowerTriangular" | custom-call | tf_op jit(solution)/shard_map/jit(_solve_triangular)/triangular_solve | solution.py:78
  246.8 24.3 %all-gather.5.cloned.1.call-done = bf16[128,16,256]{0,1,2:T(8,128)(2,1)} async-done(((bf16[128,16,64]{0,1,2:T(8,128)(2,1)}), bf16[128,16,256]{0,1,2:T(8,128)(2,1)}) %all-gather.5.cloned.1.call-update) | async-done | bytes 1048592 | tf_op jit(solution)/shard_map/all_gather | solution.py:119
  272.8 4.0 collective-permute-start.36
  276.9 3.2 collective-permute-done.35
  306.0 4.9 %collective-permute-done.37 = f32[257,128]{1,0:T(8,128)S(1)} collective-permute-done((f32[257,128]{1,0:T(8,128)S(1)}, f32[257,128]{1,0:T(8,128)S(1)}, u32[]{:S(2)}, u32[]{:S(2)}) %collective-permute-start.37) | collective-permute-done | bytes 131616 | tf_op jit(solution)/shard_map/ppermute | solution.py:40
  317.8 4.3 collective-permute-done.41
  322.1 4.9 %collective-permute-done.42 = f32[257,128]{1,0:T(8,128)S(1)} collective-permute-done((f32[257,128]{1,0:T(8,128)S(1)}, f32[257,128]{1,0:T(8,128)S(1)}, u32[]{:S(2)}, u32[]{:S(2)}) %collective-permute-start.42) | collective-permute-done | bytes 131616 | tf_op jit(solution)/shard_map/ppermute | solution.py:40
  327.8 5.0 %collective-permute-start.44 = (f32[257,128]{1,0:T(8,128)S(1)}, f32[257,128]{1,0:T(8,128)S(1)}, u32[]{:S(2)}, u32[]{:S(2)}) collective-permute-start(f32[257,128]{1,0:T(8,128)S(1)} %select_reduce_fusion.1), channel_id=1, source_target_pairs={{0,32},{4,36},{8,40},{12,44},{16,48},{20,52},{24,56},{28,60},{32,0... | collective-permute-start | bytes 394760 | tf_op jit(solution)/shard_map/ppermute | solution.py:29
  332.8 4.1 collective-permute-done.44
  358.6 6.5 %collective-permute-start.52 = (f32[128,128]{1,0:T(8,128)S(1)}, f32[128,128]{1,0:T(8,128)S(1)}, u32[]{:S(2)}, u32[]{:S(2)}) collective-permute-start(f32[128,128]{1,0:T(8,128)S(1)} %add.231), channel_id=1, source_target_pairs={{0,8},{4,12},{8,16},{12,20},{16,24},{20,28},{24,0},{28,4},{32,40},... | collective-permute-start | bytes 196616 | tf_op jit(solution)/shard_map/ppermute | solution.py:40
  367.6 3.6 collective-permute-done.53
  371.9 4.2 collective-permute-start.55
  376.1 4.0 collective-permute-done.55
  388.5 11.7 %cholesky.81 = f32[128,128]{1,0:T(8,128)S(1)} custom-call(f32[128,128]{1,0:T(8,128)S(1)} %fusion.118), custom_call_target="Cholesky" | custom-call | tf_op jit(solution)/shard_map/jit(cholesky)/cholesky | solution.py:76
  401.5 9.8 %custom-call.9 = f32[1,128,128]{1,2,0:T(8,128)S(1)} custom-call(f32[1,128,128]{2,1,0:T(8,128)S(1)} %fusion.116), custom_call_target="InvertDiagBlocksLowerTriangular" | custom-call | tf_op jit(solution)/shard_map/jit(_solve_triangular)/triangular_solve | solution.py:78
  428.3 4.9 %collective-permute-start.66 = (f32[128]{0:T(128)S(1)}, f32[128]{0:T(128)S(1)}, u32[]{:S(2)}, u32[]{:S(2)}) collective-permute-start(f32[128]{0:T(128)S(1)} %select_reduce_fusion.17), channel_id=1, source_target_pairs={{0,32},{4,36},{8,40},{12,44},{16,48},{20,52},{24,56},{28,60},{32,0... | collective-permute-start | bytes 1544 | tf_op jit(solution)/shard_map/ppermute | solution.py:29
  443.0 3.9 all-to-all-start.1
  448.2 5.4 %all-to-all-done.1 = bf16[4,2,16384]{2,1,0:T(2,128)(2,1)S(1)} async-done(((bf16[4,2,16384]{2,1,0:T(2,128)(2,1)}), bf16[4,2,16384]{2,1,0:T(2,128)(2,1)S(1)}, u32[]{:S(2)}, u32[]{:S(2)}) %all-to-all-start.1) | async-done | bytes 262176 | tf_op jit(solution)/shard_map/all_to_all | solution.py:144
  (325 shorter events, 221.6 us)
Async XLA Ops:
  11.2 11.0 %all-to-all-start = ((bf16[4,2,16384]{2,1,0:T(2,128)(2,1)}), bf16[4,2,16384]{2,1,0:T(2,128)(2,1)S(1)}, u32[]{:S(2)}, u32[]{:S(2)}) async-start(bf16[4,2,16384]{2,1,0:T(2,128)(2,1)} %reshape.448), calls=%async_computation | async-start | bytes 524288 | tf_op jit(solution)/shard_map/all_to_all | solution.py:105
  15.5 99.6 %all-gather.3.cloned.1.call-start = ((), (), s32[]{:S(2)}) async-start(), calls=%async_computation.2 | async-start | bytes 1310720 | tf_op jit(solution)/shard_map/all_gather | solution.py:119
  33.4 7.6 %collective-permute-start.4 = (f32[128,128]{1,0:T(8,128)S(1)}, f32[128,128]{1,0:T(8,128)S(1)}, u32[]{:S(2)}, u32[]{:S(2)}) collective-permute-start(f32[128,128]{1,0:T(8,128)S(1)} %add.200), channel_id=1, source_target_pairs={{0,8},{4,12},{8,16},{12,20},{16,24},{20,28},{24,0},{28,4},{32,40},... | collective-permute-start | bytes 196616 | tf_op jit(solution)/shard_map/ppermute | solution.py:40
  35.3 8.0 %collective-permute-start.5 = (f32[128,128]{1,0:T(8,128)S(1)}, f32[128,128]{1,0:T(8,128)S(1)}, u32[]{:S(2)}, u32[]{:S(2)}) collective-permute-start(f32[128,128]{1,0:T(8,128)S(1)} %add.200), channel_id=1, source_target_pairs={{0,16},{4,20},{8,24},{12,28},{16,0},{20,4},{24,8},{28,12},{32,48},... | collective-permute-start | bytes 196616 | tf_op jit(solution)/shard_map/ppermute | solution.py:40
  44.5 8.3 %collective-permute-start.7 = (f32[128,128]{1,0:T(8,128)S(1)}, f32[128,128]{1,0:T(8,128)S(1)}, u32[]{:S(2)}, u32[]{:S(2)}) collective-permute-start(f32[128,128]{1,0:T(8,128)S(1)} %select_reduce_fusion.13), channel_id=1, source_target_pairs={{0,32},{4,36},{8,40},{12,44},{16,48},{20,52},{24,56},{28,60},{32,0... | collective-permute-start | bytes 196616 | tf_op jit(solution)/shard_map/ppermute | solution.py:29
  85.8 185.3 %all-gather.5.cloned.1.call-start = ((), (), s32[]{:S(2)}) async-start(), calls=%async_computation.3 | async-start | bytes 1310720 | tf_op jit(solution)/shard_map/all_gather | solution.py:119
  116.8 7.3 %collective-permute-start.11 = (bf16[128,3,256]{2,0,1:T(8,128)(2,1)S(1)}, bf16[128,3,256]{2,0,1:T(8,128)(2,1)S(1)}, u32[]{:S(2)}, u32[]{:S(2)}) collective-permute-start(bf16[128,3,256]{2,0,1:T(8,128)(2,1)S(1)} %get-tuple-element.27), channel_id=1, source_target_pairs={{0,4},{4,8},{8,12},{12,16},{16,20},{20,24},{24,28},{28,32},{32,36}... | collective-permute-start | bytes 589832 | tf_op jit(solution)/shard_map/ppermute | solution.py:18
  116.9 7.2 %collective-permute-start.12 = (bf16[128,3,256]{2,0,1:T(8,128)(2,1)S(1)}, bf16[128,3,256]{2,0,1:T(8,128)(2,1)S(1)}, u32[]{:S(2)}, u32[]{:S(2)}) collective-permute-start(bf16[128,3,256]{2,0,1:T(8,128)(2,1)S(1)} %get-tuple-element.28), channel_id=1, source_target_pairs={{4,0},{8,4},{12,8},{16,12},{20,16},{24,20},{28,24},{32,28},{36,32}... | collective-permute-start | bytes 589832 | tf_op jit(solution)/shard_map/ppermute | solution.py:20
  145.2 6.9 %collective-permute-start.13 = (f32[129,128]{1,0:T(8,128)S(1)}, f32[129,128]{1,0:T(8,128)S(1)}, u32[]{:S(2)}, u32[]{:S(2)}) collective-permute-start(f32[129,128]{1,0:T(8,128)S(1)} %get-tuple-element.34), channel_id=1, source_target_pairs={{0,1},{1,2},{2,3},{3,0},{4,5},{5,6},{6,7},{7,4},{8,9},{9,10},{10,1... | collective-permute-start | bytes 198152 | tf_op jit(solution)/shard_map/ppermute | solution.py:40
  154.7 7.0 %collective-permute-start.17 = (f32[129,128]{1,0:T(8,128)S(1)}, f32[129,128]{1,0:T(8,128)S(1)}, u32[]{:S(2)}, u32[]{:S(2)}) collective-permute-start(f32[129,128]{1,0:T(8,128)S(1)} %add.217), channel_id=1, source_target_pairs={{0,8},{4,12},{8,16},{12,20},{16,24},{20,28},{24,0},{28,4},{32,40},... | collective-permute-start | bytes 198152 | tf_op jit(solution)/shard_map/ppermute | solution.py:40
  154.9 9.3 %collective-permute-start.18 = (f32[129,128]{1,0:T(8,128)S(1)}, f32[129,128]{1,0:T(8,128)S(1)}, u32[]{:S(2)}, u32[]{:S(2)}) collective-permute-start(f32[129,128]{1,0:T(8,128)S(1)} %add.217), channel_id=1, source_target_pairs={{0,16},{4,20},{8,24},{12,28},{16,0},{20,4},{24,8},{28,12},{32,48},... | collective-permute-start | bytes 198152 | tf_op jit(solution)/shard_map/ppermute | solution.py:40
  165.2 9.0 %collective-permute-start.20 = (f32[129,128]{1,0:T(8,128)S(1)}, f32[129,128]{1,0:T(8,128)S(1)}, u32[]{:S(2)}, u32[]{:S(2)}) collective-permute-start(f32[129,128]{1,0:T(8,128)S(1)} %select_reduce_fusion.4), channel_id=1, source_target_pairs={{0,32},{4,36},{8,40},{12,44},{16,48},{20,52},{24,56},{28,60},{32,0... | collective-permute-start | bytes 198152 | tf_op jit(solution)/shard_map/ppermute | solution.py:29
  194.3 6.9 %collective-permute-start.28 = (f32[128,128]{1,0:T(8,128)S(1)}, f32[128,128]{1,0:T(8,128)S(1)}, u32[]{:S(2)}, u32[]{:S(2)}) collective-permute-start(f32[128,128]{1,0:T(8,128)S(1)} %add.219), channel_id=1, source_target_pairs={{0,8},{4,12},{8,16},{12,20},{16,24},{20,28},{24,0},{28,4},{32,40},... | collective-permute-start | bytes 196616 | tf_op jit(solution)/shard_map/ppermute | solution.py:40
  195.8 7.4 %collective-permute-start.29 = (f32[128,128]{1,0:T(8,128)S(1)}, f32[128,128]{1,0:T(8,128)S(1)}, u32[]{:S(2)}, u32[]{:S(2)}) collective-permute-start(f32[128,128]{1,0:T(8,128)S(1)} %add.219), channel_id=1, source_target_pairs={{0,16},{4,20},{8,24},{12,28},{16,0},{20,4},{24,8},{28,12},{32,48},... | collective-permute-start | bytes 196616 | tf_op jit(solution)/shard_map/ppermute | solution.py:40
  203.9 9.0 %collective-permute-start.31 = (f32[128,128]{1,0:T(8,128)S(1)}, f32[128,128]{1,0:T(8,128)S(1)}, u32[]{:S(2)}, u32[]{:S(2)}) collective-permute-start(f32[128,128]{1,0:T(8,128)S(1)} %select_reduce_fusion.10), channel_id=1, source_target_pairs={{0,32},{4,36},{8,40},{12,44},{16,48},{20,52},{24,56},{28,60},{32,0... | collective-permute-start | bytes 196616 | tf_op jit(solution)/shard_map/ppermute | solution.py:29
  272.7 7.3 %collective-permute-start.35 = (bf16[128,3,256]{2,0,1:T(8,128)(2,1)S(1)}, bf16[128,3,256]{2,0,1:T(8,128)(2,1)S(1)}, u32[]{:S(2)}, u32[]{:S(2)}) collective-permute-start(bf16[128,3,256]{2,0,1:T(8,128)(2,1)S(1)} %get-tuple-element.25), channel_id=1, source_target_pairs={{0,4},{4,8},{8,12},{12,16},{16,20},{20,24},{24,28},{28,32},{32,36}... | collective-permute-start | bytes 589832 | tf_op jit(solution)/shard_map/ppermute | solution.py:18
  272.8 7.2 %collective-permute-start.36 = (bf16[128,3,256]{2,0,1:T(8,128)(2,1)S(1)}, bf16[128,3,256]{2,0,1:T(8,128)(2,1)S(1)}, u32[]{:S(2)}, u32[]{:S(2)}) collective-permute-start(bf16[128,3,256]{2,0,1:T(8,128)(2,1)S(1)} %get-tuple-element.26), channel_id=1, source_target_pairs={{4,0},{8,4},{12,8},{16,12},{20,16},{24,20},{28,24},{32,28},{36,32}... | collective-permute-start | bytes 589832 | tf_op jit(solution)/shard_map/ppermute | solution.py:20
  301.2 9.7 %collective-permute-start.37 = (f32[257,128]{1,0:T(8,128)S(1)}, f32[257,128]{1,0:T(8,128)S(1)}, u32[]{:S(2)}, u32[]{:S(2)}) collective-permute-start(f32[257,128]{1,0:T(8,128)S(1)} %get-tuple-element.32), channel_id=1, source_target_pairs={{0,1},{1,2},{2,3},{3,0},{4,5},{5,6},{6,7},{7,4},{8,9},{9,10},{10,1... | collective-permute-start | bytes 394760 | tf_op jit(solution)/shard_map/ppermute | solution.py:40
  301.6 9.3 %collective-permute-start.38 = (f32[257,128]{1,0:T(8,128)S(1)}, f32[257,128]{1,0:T(8,128)S(1)}, u32[]{:S(2)}, u32[]{:S(2)}) collective-permute-start(f32[257,128]{1,0:T(8,128)S(1)} %get-tuple-element.32), channel_id=1, source_target_pairs={{0,2},{1,3},{2,0},{3,1},{4,6},{5,7},{6,4},{7,5},{8,10},{9,11},{10,... | collective-permute-start | bytes 394760 | tf_op jit(solution)/shard_map/ppermute | solution.py:40
  304.3 7.2 %collective-permute-start.39 = (f32[257,128]{1,0:T(8,128)S(1)}, f32[257,128]{1,0:T(8,128)S(1)}, u32[]{:S(2)}, u32[]{:S(2)}) collective-permute-start(f32[257,128]{1,0:T(8,128)S(1)} %get-tuple-element.32), channel_id=1, source_target_pairs={{0,3},{1,0},{2,1},{3,2},{4,7},{5,4},{6,5},{7,6},{8,11},{9,8},{10,9... | collective-permute-start | bytes 394760 | tf_op jit(solution)/shard_map/ppermute | solution.py:40
  313.7 8.4 %collective-permute-start.41 = (f32[257,128]{1,0:T(8,128)S(1)}, f32[257,128]{1,0:T(8,128)S(1)}, u32[]{:S(2)}, u32[]{:S(2)}) collective-permute-start(f32[257,128]{1,0:T(8,128)S(1)} %add.229), channel_id=1, source_target_pairs={{0,8},{4,12},{8,16},{12,20},{16,24},{20,28},{24,0},{28,4},{32,40},... | collective-permute-start | bytes 394760 | tf_op jit(solution)/shard_map/ppermute | solution.py:40
  313.9 13.1 %collective-permute-start.42 = (f32[257,128]{1,0:T(8,128)S(1)}, f32[257,128]{1,0:T(8,128)S(1)}, u32[]{:S(2)}, u32[]{:S(2)}) collective-permute-start(f32[257,128]{1,0:T(8,128)S(1)} %add.229), channel_id=1, source_target_pairs={{0,16},{4,20},{8,24},{12,28},{16,0},{20,4},{24,8},{28,12},{32,48},... | collective-permute-start | bytes 394760 | tf_op jit(solution)/shard_map/ppermute | solution.py:40
  316.6 10.5 %collective-permute-start.43 = (f32[257,128]{1,0:T(8,128)S(1)}, f32[257,128]{1,0:T(8,128)S(1)}, u32[]{:S(2)}, u32[]{:S(2)}) collective-permute-start(f32[257,128]{1,0:T(8,128)S(1)} %add.229), channel_id=1, source_target_pairs={{0,24},{4,28},{8,0},{12,4},{16,8},{20,12},{24,16},{28,20},{32,56},... | collective-permute-start | bytes 394760 | tf_op jit(solution)/shard_map/ppermute | solution.py:40
  327.8 9.1 %collective-permute-start.44 = (f32[257,128]{1,0:T(8,128)S(1)}, f32[257,128]{1,0:T(8,128)S(1)}, u32[]{:S(2)}, u32[]{:S(2)}) collective-permute-start(f32[257,128]{1,0:T(8,128)S(1)} %select_reduce_fusion.1), channel_id=1, source_target_pairs={{0,32},{4,36},{8,40},{12,44},{16,48},{20,52},{24,56},{28,60},{32,0... | collective-permute-start | bytes 394760 | tf_op jit(solution)/shard_map/ppermute | solution.py:29
  339.6 6.8 %collective-permute-start.47 = (f32[257,128]{1,0:T(8,128)S(1)}, f32[257,128]{1,0:T(8,128)S(1)}, u32[]{:S(2)}, u32[]{:S(2)}) collective-permute-start(f32[257,128]{1,0:T(8,128)S(1)} %add.230), channel_id=1, source_target_pairs={{0,192},{4,196},{8,200},{12,204},{16,208},{20,212},{24,216},{28,22... | collective-permute-start | bytes 394760 | tf_op jit(solution)/shard_map/ppermute | solution.py:40
  358.6 9.0 %collective-permute-start.52 = (f32[128,128]{1,0:T(8,128)S(1)}, f32[128,128]{1,0:T(8,128)S(1)}, u32[]{:S(2)}, u32[]{:S(2)}) collective-permute-start(f32[128,128]{1,0:T(8,128)S(1)} %add.231), channel_id=1, source_target_pairs={{0,8},{4,12},{8,16},{12,20},{16,24},{20,28},{24,0},{28,4},{32,40},... | collective-permute-start | bytes 196616 | tf_op jit(solution)/shard_map/ppermute | solution.py:40
  371.9 8.3 %collective-permute-start.55 = (f32[128,128]{1,0:T(8,128)S(1)}, f32[128,128]{1,0:T(8,128)S(1)}, u32[]{:S(2)}, u32[]{:S(2)}) collective-permute-start(f32[128,128]{1,0:T(8,128)S(1)} %select_reduce_fusion.7), channel_id=1, source_target_pairs={{0,32},{4,36},{8,40},{12,44},{16,48},{20,52},{24,56},{28,60},{32,0... | collective-permute-start | bytes 196616 | tf_op jit(solution)/shard_map/ppermute | solution.py:29
  428.3 7.5 %collective-permute-start.66 = (f32[128]{0:T(128)S(1)}, f32[128]{0:T(128)S(1)}, u32[]{:S(2)}, u32[]{:S(2)}) collective-permute-start(f32[128]{0:T(128)S(1)} %select_reduce_fusion.17), channel_id=1, source_target_pairs={{0,32},{4,36},{8,40},{12,44},{16,48},{20,52},{24,56},{28,60},{32,0... | collective-permute-start | bytes 1544 | tf_op jit(solution)/shard_map/ppermute | solution.py:29
  435.8 11.1 %collective-permute-start.67 = (f32[128]{0:T(128)S(1)}, f32[128]{0:T(128)S(1)}, u32[]{:S(2)}, u32[]{:S(2)}) collective-permute-start(f32[128]{0:T(128)S(1)} %add.234), channel_id=1, source_target_pairs={{0,64},{4,68},{8,72},{12,76},{16,80},{20,84},{24,88},{28,92},{32,9... | collective-permute-start | bytes 1544 | tf_op jit(solution)/shard_map/ppermute | solution.py:40
  436.7 10.1 %collective-permute-start.68 = (f32[128]{0:T(128)S(1)}, f32[128]{0:T(128)S(1)}, u32[]{:S(2)}, u32[]{:S(2)}) collective-permute-start(f32[128]{0:T(128)S(1)} %add.234), channel_id=1, source_target_pairs={{0,128},{4,132},{8,136},{12,140},{16,144},{20,148},{24,152},{28,15... | collective-permute-start | bytes 1544 | tf_op jit(solution)/shard_map/ppermute | solution.py:40
  439.5 7.4 %collective-permute-start.69 = (f32[128]{0:T(128)S(1)}, f32[128]{0:T(128)S(1)}, u32[]{:S(2)}, u32[]{:S(2)}) collective-permute-start(f32[128]{0:T(128)S(1)} %add.234), channel_id=1, source_target_pairs={{0,192},{4,196},{8,200},{12,204},{16,208},{20,212},{24,216},{28,22... | collective-permute-start | bytes 1544 | tf_op jit(solution)/shard_map/ppermute | solution.py:40
  443.0 10.6 %all-to-all-start.1 = ((bf16[4,2,16384]{2,1,0:T(2,128)(2,1)}), bf16[4,2,16384]{2,1,0:T(2,128)(2,1)S(1)}, u32[]{:S(2)}, u32[]{:S(2)}) async-start(bf16[4,2,16384]{2,1,0:T(2,128)(2,1)} %reshape.450), calls=%async_computation.1 | async-start | bytes 524288 | tf_op jit(solution)/shard_map/all_to_all | solution.py:144
  (55 other events, 304.2 us)
Sparse Core Ops, SparseCore 0:
  85.9 29.1 all-gather.2
  246.9 24.1 all-gather.4
